TPU v7x, 256 devices: a whole 4x4x8 slice. The times are simulated.
256 devices in a mesh: leaf: 4 (over y), row: 8 (over z), col: 8 (over x, core).
Axes of the slice: x: 4, y: 4, z: 8, core: 2. Of those that a mesh axis runs over, the one named last changes fastest.
Arguments:
- rhs: float32 [4, 4, 8, 256, 256], P('leaf', None, 'row'), may hold values from -6 to 6
- rhs_top: float32 [2, 8, 256, 256], P(None, 'row'), may hold values from -6 to 6
- factor: bfloat16 [4, 4, 8, 4, 8, 256, 256], P('leaf', None, 'row', None, 'col'), may hold values from -0.125 to 0.125
- factor_inv: bfloat16 [4, 2, 4, 8, 256, 256], P('leaf', None, None, 'row')
- lower_bridge: bfloat16 [4, 2, 8, 4, 8, 256, 256], P('leaf', None, 'row', None, 'col'), may hold values from -0.0625 to 0.0625
- upper_bridge: bfloat16 [4, 4, 8, 2, 8, 256, 256], P('leaf', None, 'row', None, 'col'), may hold values from -0.1875 to 0.1875
- top_factor: bfloat16 [2, 8, 2, 8, 256, 256], P(None, 'row', None, 'col'), may hold values from -0.1875 to 0.1875
- top_inv: bfloat16 [2, 2, 8, 256, 256], P(None, None, 'row')
- widths: int32 [4, 4, 8], P('leaf', None, 'row'), may hold values from 128 to 256, as said below
- pattern: int32 [4, 4, 8, 4, 8], P('leaf', None, 'row', None, 'col'), may hold values 0 or 1
- lower_links: int32 [4, 2, 8, 4, 8], P('leaf', None, 'row', None, 'col'), may hold values 0 or 1
- upper_links: int32 [4, 4, 8, 2, 8], P('leaf', None, 'row', None, 'col'), may hold values 0 or 1
- top_pattern: int32 [2, 8, 2, 8], P(None, 'row', None, 'col'), may hold values 0 or 1
Outputs:
- solution: float32 [4, 4, 8, 256, 256], P('leaf', None, 'row', None, 'col')
- solution_top: float32 [2, 8, 256, 256], P(None, 'row', None, 'col')
Inputs may be any that keep to these rules, and one draw needn't show every extreme that they name: widths of supernodes; the largest is 256 in every subtree.
All inputs are finite; a program needn't handle non-finite values. No bound on the sum of `pattern` or of `lower_links` or of `upper_links` or of `top_pattern` on one device may be relied on, other than what follows from the above.
Results may differ from a plain program's by a relative error of at most 0.02.
Values may be sent and summed in bfloat16 or wider, within the bound.
No kernel may reach another device: no remote copies, remote signals or barrier semaphores. Data moves between devices by JAX's collectives and lax.ppermute only.
A program may use at most 64 MiB of HBM per device.

v0:
```python
import jax
import jax.numpy as jnp
from jax import lax
from jax.sharding import PartitionSpec as P


def masked(blocks, marks):
    return blocks * marks.astype(jnp.bfloat16)[..., None, None]


def column_part(full, width):
    start = lax.axis_index("col") * width
    return lax.dynamic_slice_in_dim(full, start, width, 0)


def settle(partial_value, target, inverse, keep):
    share = lax.psum_scatter(partial_value, "col", scatter_dimension=2, tiled=True)
    resid = (target - share).astype(jnp.bfloat16)
    solved = keep * jnp.einsum("ibk,ikr->ibr", inverse, resid, preferred_element_type=jnp.float32)
    pieces = lax.all_gather(solved.astype(jnp.bfloat16)[None], ("row", "col"), axis=0, tiled=True)
    nrows = lax.axis_size("row")
    ncols = lax.axis_size("col")
    pieces = pieces.reshape((nrows, ncols) + solved.shape)
    full = jnp.transpose(pieces, (0, 2, 3, 1, 4)).reshape(
        nrows * solved.shape[0], solved.shape[1], ncols * solved.shape[2]
    )
    return (solved, full)


def shards(
    rhs,
    rhs_top,
    factor,
    factor_inv,
    lower_bridge,
    upper_bridge,
    top_factor,
    top_inv,
    widths,
    pattern,
    lower_links,
    upper_links,
    top_pattern,
):
    f32 = jnp.float32
    levels = factor.shape[1]
    tops = top_factor.shape[0]
    row_count = factor.shape[2]
    col_count = factor.shape[4]
    block = factor.shape[5]
    sides = rhs.shape[4]
    share_width = sides // lax.axis_size("col")
    col_start = lax.axis_index("col") * share_width
    local_rhs = lax.dynamic_slice_in_dim(rhs[0], col_start, share_width, 3)
    local_top = lax.dynamic_slice_in_dim(rhs_top, col_start, share_width, 3)
    fmask = masked(factor[0], pattern[0])
    lmask = masked(lower_bridge[0], lower_links[0])
    umask = masked(upper_bridge[0], upper_links[0])
    tmask = masked(top_factor, top_pattern)
    marks = lax.broadcasted_iota(jnp.int32, (levels, row_count, block, 1), 2)
    keep = (marks < widths[0][..., None, None]).astype(f32)
    ys = []
    ycols = []
    for level in range(levels):
        if level == 0:
            partial_value = jnp.zeros((row_count, block, sides), f32)
        else:
            partial_value = jnp.einsum(
                "iljbk,ljkr->ibr",
                fmask[level, :, :level],
                jnp.stack(ycols, 0),
                preferred_element_type=f32,
            )
        solved, full = settle(partial_value, local_rhs[level], factor_inv[0, 0, level], keep[level])
        ys.append(solved)
        ycols.append(column_part(full, col_count))
    coupling = jnp.einsum(
        "tiljbk,ljkr->tibr", lmask, jnp.stack(ycols, 0), preferred_element_type=f32
    )
    coupling = lax.psum(coupling, "leaf")
    yts = []
    tcols = []
    for top in range(tops):
        partial_value = coupling[top]
        if top > 0:
            partial_value = partial_value + jnp.einsum(
                "iljbk,ljkr->ibr",
                tmask[top, :, :top],
                jnp.stack(tcols, 0),
                preferred_element_type=f32,
            )
        solved, full = settle(partial_value, local_top[top], top_inv[0, top], 1.0)
        yts.append(solved)
        tcols.append(column_part(full, col_count))
    zts = [None] * tops
    zt_cols = [None] * tops
    for top in reversed(range(tops)):
        if top == tops - 1:
            partial_value = jnp.zeros((row_count, block, sides), f32)
        else:
            partial_value = jnp.einsum(
                "iljbk,ljkr->ibr",
                tmask[top, :, top + 1 :],
                jnp.stack(zt_cols[top + 1 :], 0),
                preferred_element_type=f32,
            )
        solved, full = settle(partial_value, yts[top], top_inv[1, top], 1.0)
        zts[top] = solved
        zt_cols[top] = column_part(full, col_count)
    top_stack = jnp.stack(zt_cols, 0)
    zs = [None] * levels
    zcols = [None] * levels
    for level in reversed(range(levels)):
        partial_value = jnp.einsum(
            "itjbk,tjkr->ibr", umask[level], top_stack, preferred_element_type=f32
        )
        if level < levels - 1:
            partial_value = partial_value + jnp.einsum(
                "iljbk,ljkr->ibr",
                fmask[level, :, level + 1 :],
                jnp.stack(zcols[level + 1 :], 0),
                preferred_element_type=f32,
            )
        solved, full = settle(partial_value, ys[level], factor_inv[0, 1, level], keep[level])
        zs[level] = solved
        zcols[level] = column_part(full, col_count)
    result = jnp.stack(zs, 0)
    result_top = jnp.stack(zts, 0)
    return (result[None], result_top)


def solution(mesh):
    placed = (
        P("leaf", None, "row", None, None),
        P(None, "row", None, None),
        P("leaf", None, "row", None, "col", None, None),
        P("leaf", None, None, "row", None, None),
        P("leaf", None, "row", None, "col", None, None),
        P("leaf", None, "row", None, "col", None, None),
        P(None, "row", None, "col", None, None),
        P(None, None, "row", None, None),
        P("leaf", None, "row"),
        P("leaf", None, "row", None, "col"),
        P("leaf", None, "row", None, "col"),
        P("leaf", None, "row", None, "col"),
        P(None, "row", None, "col"),
    )
    return jax.shard_map(
        shards,
        mesh=mesh,
        in_specs=placed,
        out_specs=(P("leaf", None, "row", None, "col"), P(None, "row", None, "col")),
        check_vma=False,
    )
```

profile of v0, /device:TPU:8, one launch (start us, length us, event | category | flops | bytes accessed | tf_op | source)
XLA Modules:
  0.0 1329.3 jit_solution(12221357856252894785)
XLA Ops:
  7.2 1.2 copy-done
  9.5 1.7 bitcast_convert_fusion.9
  12.0 1.8 bitcast_multiply_fusion
  13.8 70.6 %all-gather.21.cloned.1.call-done = bf16[16384,32]{0,1:T(8,128)(2,1)} async-done(((bf16[256,32]{0,1:T(8,128)(2,1)}), bf16[16384,32]{0,1:T(8,128)(2,1)}) %all-gather.21.cloned.1.call-update) | async-done | bytes 1048592 | tf_op jit(solution)/shard_map/all_gather | solution.py:20
  84.4 1.5 copy.160
  87.6 1.7 fusion.99
  89.4 1.6 copy.157
  90.9 1.3 dynamic-slice.1
  92.9 59.3 %all-reduce.14.cloned.1.call-done = f32[1,256,256]{1,0,2:T(1,128)} async-done(((f32[1,256,256]{1,0,2:T(1,128)}), f32[1,256,256]{1,0,2:T(1,128)}) %all-reduce.14.cloned.1.call-update) | async-done | bytes 262160
  153.0 1.7 bitcast_convert_fusion.8
  155.5 69.2 %all-gather.23.cloned.1.call-done = bf16[16384,32]{0,1:T(8,128)(2,1)} async-done(((bf16[256,32]{0,1:T(8,128)(2,1)}), bf16[16384,32]{0,1:T(8,128)(2,1)}) %all-gather.23.cloned.1.call-update) | async-done | bytes 1048592 | tf_op jit(solution)/shard_map/all_gather | solution.py:20
  224.7 1.5 copy.161
  227.6 1.9 convolution_bitcast_fusion.8
  229.5 1.8 copy.101
  231.4 64.5 %all-reduce.16.cloned.1.call-done = f32[1,256,256]{1,0,2:T(1,128)} async-done(((f32[1,256,256]{1,0,2:T(1,128)}), f32[1,256,256]{1,0,2:T(1,128)}) %all-reduce.16.cloned.1.call-update) | async-done | bytes 262160
  296.6 1.7 bitcast_convert_fusion.7
  298.4 69.4 %all-gather.25.cloned.1.call-done = bf16[16384,32]{0,1:T(8,128)(2,1)} async-done(((bf16[256,32]{0,1:T(8,128)(2,1)}), bf16[16384,32]{0,1:T(8,128)(2,1)}) %all-gather.25.cloned.1.call-update) | async-done | bytes 1048592 | tf_op jit(solution)/shard_map/all_gather | solution.py:20
  367.8 1.5 copy.162
  370.7 2.0 convolution_bitcast_fusion.7
  372.6 1.8 copy.105
  374.6 64.5 %all-reduce.18.cloned.1.call-done = f32[1,256,256]{1,0,2:T(1,128)} async-done(((f32[1,256,256]{1,0,2:T(1,128)}), f32[1,256,256]{1,0,2:T(1,128)}) %all-reduce.18.cloned.1.call-update) | async-done | bytes 262160
  439.8 1.7 bitcast_convert_fusion.6
  442.8 68.2 %all-gather.27.cloned.1.call-done = bf16[16384,32]{0,1:T(8,128)(2,1)} async-done(((bf16[256,32]{0,1:T(8,128)(2,1)}), bf16[16384,32]{0,1:T(8,128)(2,1)}) %all-gather.27.cloned.1.call-update) | async-done | bytes 1048592 | tf_op jit(solution)/shard_map/all_gather | solution.py:20
  511.0 1.5 copy.163
  513.9 2.6 convolution_bitcast_fusion
  516.5 46.4 %all-reduce.12.cloned.1.call-done = f32[2,1,256,256]{3,2,0,1:T(8,128)} async-done(((f32[2,1,256,256]{3,2,0,1:T(8,128)}), f32[2,1,256,256]{3,2,0,1:T(8,128)}) %all-reduce.12.cloned.1.call-update) | async-done | bytes 524304 | tf_op jit(solution)/shard_map/psum | solution.py:80
  564.8 1.1 constant_dynamic-slice_fusion.10
  566.0 66.3 %all-reduce.20.cloned.1.call-done = f32[1,256,256]{1,0,2:T(1,128)} async-done(((f32[1,256,256]{1,0,2:T(1,128)}), f32[1,256,256]{1,0,2:T(1,128)}) %all-reduce.20.cloned.1.call-update) | async-done | bytes 262160
  633.0 1.7 bitcast_convert_fusion.5
  635.5 1.9 broadcast_multiply_fusion
  637.5 66.7 %all-gather.29.cloned.1.call-done = bf16[16384,32]{0,1:T(8,128)(2,1)} async-done(((bf16[256,32]{0,1:T(8,128)(2,1)}), bf16[16384,32]{0,1:T(8,128)(2,1)}) %all-gather.29.cloned.1.call-update) | async-done | bytes 1048592 | tf_op jit(solution)/shard_map/all_gather | solution.py:20
  704.2 1.5 copy.164
  706.3 1.1 fusion.1
  708.4 64.5 %all-reduce.22.cloned.1.call-done = f32[1,256,256]{1,0,2:T(1,128)} async-done(((f32[1,256,256]{1,0,2:T(1,128)}), f32[1,256,256]{1,0,2:T(1,128)}) %all-reduce.22.cloned.1.call-update) | async-done | bytes 262160
  773.7 1.9 bitcast_convert_fusion.4
  775.7 69.4 %all-gather.31.cloned.1.call-done = bf16[16384,32]{0,1:T(8,128)(2,1)} async-done(((bf16[256,32]{0,1:T(8,128)(2,1)}), bf16[16384,32]{0,1:T(8,128)(2,1)}) %all-gather.31.cloned.1.call-update) | async-done | bytes 1048592 | tf_op jit(solution)/shard_map/all_gather | solution.py:20
  845.1 1.5 copy.165
  847.2 1.8 convolution_bitcast_fusion.9
  849.1 32.6 %reduce-scatter.6.cloned.1.call-done = f32[1,256,32]{1,2,0:T(8,128)} async-done(((f32[1,256,256]{1,2,0:T(8,128)}), f32[1,256,32]{1,2,0:T(8,128)}) %reduce-scatter.6.cloned.1.call-update) | async-done | bytes 32784 | tf_op jit(solution)/shard_map/reduce_scatter | solution.py:17
  881.7 1.7 bitcast_convert_fusion.3
  883.6 2.4 bitcast_multiply_fusion.3
  886.1 67.7 %all-gather.33.cloned.1.call-done = bf16[16384,32]{0,1:T(8,128)(2,1)} async-done(((bf16[256,32]{0,1:T(8,128)(2,1)}), bf16[16384,32]{0,1:T(8,128)(2,1)}) %all-gather.33.cloned.1.call-update) | async-done | bytes 1048592 | tf_op jit(solution)/shard_map/all_gather | solution.py:20
  953.8 1.5 copy.166
  956.0 1.9 convolution_bitcast_fusion.3
  958.0 32.6 %reduce-scatter.8.cloned.1.call-done = f32[1,256,32]{1,2,0:T(8,128)} async-done(((f32[1,256,256]{1,2,0:T(8,128)}), f32[1,256,32]{1,2,0:T(8,128)}) %reduce-scatter.8.cloned.1.call-update) | async-done | bytes 32784 | tf_op jit(solution)/shard_map/reduce_scatter | solution.py:17
  990.7 1.7 bitcast_convert_fusion.2
  992.7 2.0 convolution_bitcast_fusion.4
  994.6 68.2 %all-gather.35.cloned.1.call-done = bf16[16384,32]{0,1:T(8,128)(2,1)} async-done(((bf16[256,32]{0,1:T(8,128)(2,1)}), bf16[16384,32]{0,1:T(8,128)(2,1)}) %all-gather.35.cloned.1.call-update) | async-done | bytes 1048592 | tf_op jit(solution)/shard_map/all_gather | solution.py:20
  1062.8 1.5 copy.167
  1066.0 32.6 %reduce-scatter.10.cloned.1.call-done = f32[1,256,32]{1,2,0:T(8,128)} async-done(((f32[1,256,256]{1,2,0:T(8,128)}), f32[1,256,32]{1,2,0:T(8,128)}) %reduce-scatter.10.cloned.1.call-update) | async-done | bytes 32784 | tf_op jit(solution)/shard_map/reduce_scatter | solution.py:17
  1098.6 1.7 bitcast_convert_fusion.1
  1101.1 69.0 %all-gather.37.cloned.1.call-done = bf16[16384,32]{0,1:T(8,128)(2,1)} async-done(((bf16[256,32]{0,1:T(8,128)(2,1)}), bf16[16384,32]{0,1:T(8,128)(2,1)}) %all-gather.37.cloned.1.call-update) | async-done | bytes 1048592 | tf_op jit(solution)/shard_map/all_gather | solution.py:20
  1170.1 1.5 copy.168
  1173.0 1.2 convolution_bitcast_fusion.2
  1174.2 2.0 fusion.5
  1176.3 32.6 %reduce-scatter.12.cloned.1.call-done = f32[1,256,32]{1,2,0:T(8,128)} async-done(((f32[1,256,256]{1,2,0:T(8,128)}), f32[1,256,32]{1,2,0:T(8,128)}) %reduce-scatter.12.cloned.1.call-update) | async-done | bytes 32784 | tf_op jit(solution)/shard_map/reduce_scatter | solution.py:17
  1208.9 1.7 bitcast_convert_fusion
  1210.7 70.3 %all-gather.39.cloned.1.call-done = bf16[16384,32]{0,1:T(8,128)(2,1)} async-done(((bf16[256,32]{0,1:T(8,128)(2,1)}), bf16[16384,32]{0,1:T(8,128)(2,1)}) %all-gather.39.cloned.1.call-update) | async-done | bytes 1048592 | tf_op jit(solution)/shard_map/all_gather | solution.py:20
  1281.0 1.5 copy.169
  1283.9 1.4 convolution_bitcast_fusion.1
  1285.3 1.9 fusion.3
  1287.9 32.0 %reduce-scatter.14.cloned.1.call-done = f32[1,256,32]{1,2,0:T(8,128)} async-done(((f32[1,256,256]{1,2,0:T(8,128)}), f32[1,256,32]{1,2,0:T(8,128)}) %reduce-scatter.14.cloned.1.call-update) | async-done | bytes 32784 | tf_op jit(solution)/shard_map/reduce_scatter | solution.py:17
  1319.9 1.1 fusion.6
  1321.0 1.5 maximum_bitcast_fusion.11
  (124 shorter events, 26.1 us)
Async XLA Ops:
  7.2 1.2 copy-start
  7.2 77.2 %all-gather.21.cloned.1.call-start = ((), (), s32[]{:S(2)}) async-start(), calls=%async_computation.11 | async-start | bytes 1064960 | tf_op jit(solution)/shard_map/all_gather | solution.py:20
  8.6 3.4 copy-start.1
  11.2 141.0 %all-reduce.14.cloned.1.call-start = ((), (), s32[]{:S(2)}) async-start(), calls=%async_computation.21 | async-start | bytes 524288
  87.6 137.1 %all-gather.23.cloned.1.call-start = ((), (), s32[]{:S(2)}) async-start(), calls=%async_computation.12 | async-start | bytes 1064960 | tf_op jit(solution)/shard_map/all_gather | solution.py:20
  154.7 141.2 %all-reduce.16.cloned.1.call-start = ((), (), s32[]{:S(2)}) async-start(), calls=%async_computation.22 | async-start | bytes 524288
  231.3 136.5 %all-gather.25.cloned.1.call-start = ((), (), s32[]{:S(2)}) async-start(), calls=%async_computation.13 | async-start | bytes 1064960 | tf_op jit(solution)/shard_map/all_gather | solution.py:20
  298.4 140.7 %all-reduce.18.cloned.1.call-start = ((), (), s32[]{:S(2)}) async-start(), calls=%async_computation.23 | async-start | bytes 524288
  367.8 2.9 copy-start.6
  374.5 136.5 %all-gather.27.cloned.1.call-start = ((), (), s32[]{:S(2)}) async-start(), calls=%async_computation.14 | async-start | bytes 1064960 | tf_op jit(solution)/shard_map/all_gather | solution.py:20
  441.5 121.4 %all-reduce.12.cloned.1.call-start = ((), (), s32[]{:S(2)}) async-start(), calls=%async_computation.5 | async-start | bytes 1048576 | tf_op jit(solution)/shard_map/psum | solution.py:80
  511.0 2.9 copy-start.7
  516.5 115.8 %all-reduce.20.cloned.1.call-start = ((), (), s32[]{:S(2)}) async-start(), calls=%async_computation.24 | async-start | bytes 524288
  564.7 139.4 %all-gather.29.cloned.1.call-start = ((), (), s32[]{:S(2)}) async-start(), calls=%async_computation.15 | async-start | bytes 1064960 | tf_op jit(solution)/shard_map/all_gather | solution.py:20
  634.8 138.2 %all-reduce.22.cloned.1.call-start = ((), (), s32[]{:S(2)}) async-start(), calls=%async_computation.25 | async-start | bytes 524288
  704.2 2.1 copy-start.2
  708.3 136.7 %all-gather.31.cloned.1.call-start = ((), (), s32[]{:S(2)}) async-start(), calls=%async_computation.16 | async-start | bytes 1064960 | tf_op jit(solution)/shard_map/all_gather | solution.py:20
  775.6 106.1 %reduce-scatter.6.cloned.1.call-start = ((), (), s32[]{:S(2)}) async-start(), calls=%async_computation.6 | async-start | bytes 294912 | tf_op jit(solution)/shard_map/reduce_scatter | solution.py:17
  846.5 35.2 %copy-start.5 = (f32[32,256]{1,0:T(8,128)S(1)}, f32[32,256]{1,0:T(8,128)}, u32[]{:S(2)}) copy-start(f32[32,256]{1,0:T(8,128)} %get-tuple-element.28) | copy-start | bytes 98308
  846.5 37.0 %copy-start.12 = (s32[1,4,1,2,1]{1,4,3,2,0:T(1,128)S(1)}, s32[1,4,1,2,1]{1,4,3,2,0:T(1,128)}, u32[]{:S(2)}) copy-start(s32[1,4,1,2,1]{1,4,3,2,0:T(1,128)} %param.24) | copy-start | bytes 100
  849.0 104.8 %all-gather.33.cloned.1.call-start = ((), (), s32[]{:S(2)}) async-start(), calls=%async_computation.17 | async-start | bytes 1064960 | tf_op jit(solution)/shard_map/all_gather | solution.py:20
  883.4 107.2 %reduce-scatter.8.cloned.1.call-start = ((), (), s32[]{:S(2)}) async-start(), calls=%async_computation.7 | async-start | bytes 294912 | tf_op jit(solution)/shard_map/reduce_scatter | solution.py:17
  958.0 104.8 %all-gather.35.cloned.1.call-start = ((), (), s32[]{:S(2)}) async-start(), calls=%async_computation.18 | async-start | bytes 1064960 | tf_op jit(solution)/shard_map/all_gather | solution.py:20
  992.4 106.1 %reduce-scatter.10.cloned.1.call-start = ((), (), s32[]{:S(2)}) async-start(), calls=%async_computation.8 | async-start | bytes 294912 | tf_op jit(solution)/shard_map/reduce_scatter | solution.py:17
  1062.8 2.1 copy-start.3
  1065.9 104.2 %all-gather.37.cloned.1.call-start = ((), (), s32[]{:S(2)}) async-start(), calls=%async_computation.19 | async-start | bytes 1064960 | tf_op jit(solution)/shard_map/all_gather | solution.py:20
  1100.3 108.6 %reduce-scatter.12.cloned.1.call-start = ((), (), s32[]{:S(2)}) async-start(), calls=%async_computation.9 | async-start | bytes 294912 | tf_op jit(solution)/shard_map/reduce_scatter | solution.py:17
  1173.0 35.9 %copy-start.4 = (f32[32,256]{1,0:T(8,128)S(1)}, f32[32,256]{1,0:T(8,128)}, u32[]{:S(2)}) copy-start(f32[32,256]{1,0:T(8,128)} %get-tuple-element.22) | copy-start | bytes 98308
  1176.2 104.8 %all-gather.39.cloned.1.call-start = ((), (), s32[]{:S(2)}) async-start(), calls=%async_computation.20 | async-start | bytes 1064960 | tf_op jit(solution)/shard_map/all_gather | solution.py:20
  1210.6 109.3 %reduce-scatter.14.cloned.1.call-start = ((), (), s32[]{:S(2)}) async-start(), calls=%async_computation.10 | async-start | bytes 294912 | tf_op jit(solution)/shard_map/reduce_scatter | solution.py:17
  1283.9 3.4 copy-start.9
  1283.9 3.4 copy-start.10
  1283.9 36.0 %copy-start.8 = (f32[32,256]{1,0:T(8,128)S(1)}, f32[32,256]{1,0:T(8,128)}, u32[]{:S(2)}) copy-start(f32[32,256]{1,0:T(8,128)} %get-tuple-element.20) | copy-start | bytes 98308
  1283.9 37.1 %copy-start.11 = (f32[32,256]{1,0:T(8,128)S(1)}, f32[32,256]{1,0:T(8,128)}, u32[]{:S(2)}) copy-start(f32[32,256]{1,0:T(8,128)} %get-tuple-element.34) | copy-start | bytes 98308
Sparse Core Ops, SparseCore 0:
  11.3 73.0 all-gather.20
  87.7 64.4 all-reduce.13
  155.4 69.2 all-gather.22
  231.4 64.4 all-reduce.15
  298.5 69.2 all-gather.24
  374.6 64.4 all-reduce.17
  441.7 69.2 all-gather.26
  516.6 46.2 all-reduce.11
  565.2 66.9 all-reduce.19
  634.9 69.2 all-gather.28
  708.5 64.4 all-reduce.21
  775.7 69.2 all-gather.30
  849.1 32.4 reduce-scatter.5
  884.8 69.0 all-gather.32
  958.1 32.4 reduce-scatter.7
  993.7 69.0 all-gather.34
  1066.0 32.4 reduce-scatter.9
  1101.1 69.0 all-gather.36
  1176.3 32.4 reduce-scatter.11
  1212.0 69.0 all-gather.38
  1287.3 32.4 reduce-scatter.13
where the time goes:
time: 1330 us
  waiting for transfers between devices  1220 us (92%)
  local copies, waits for them, and re-layouts  45.3 us (3%)
  matrix products  39.4 us (3%)
  between operations  15.4 us (1%)
    all_gather x10, waiting for transfers between devices, settle(): lax.all_gather(solved.astype(jnp.bfloat16)[None], ('row', 'col'), axis=0,...  689 us
    unnamed x26, waiting for transfers between devices  319 us
    reduce_scatter x5, waiting for transfers between devices, settle(): lax.psum_scatter(partial_value, 'col', scatter_dimension=2, tiled=True)  162 us
    psum x1, waiting for transfers between devices, shards(): coupling = lax.psum(coupling, 'leaf')  46.4 us
  transfers between devices with their start and end apart: 21, of which 21 were waited for; matrix products, arithmetic and copies ran while one was open for 1% of the time, Pallas kernels for 0%

commit v1 on v0

--- a/solution.py
+++ b/solution.py
@@ -17,7 +17,9 @@
     share = lax.psum_scatter(partial_value, "col", scatter_dimension=2, tiled=True)
     resid = (target - share).astype(jnp.bfloat16)
     solved = keep * jnp.einsum("ibk,ikr->ibr", inverse, resid, preferred_element_type=jnp.float32)
-    pieces = lax.all_gather(solved.astype(jnp.bfloat16)[None], ("row", "col"), axis=0, tiled=True)
+    own = solved.astype(jnp.bfloat16)[None]
+    sent = jnp.stack([own] * lax.axis_size(("row", "col")))
+    pieces = jnp.concatenate(lax.all_to_all(sent, ("row", "col"), 0, 0), axis=0)
     nrows = lax.axis_size("row")
     ncols = lax.axis_size("col")
     pieces = pieces.reshape((nrows, ncols) + solved.shape)

time: 1330 us -> 970 us (0.73)
  waiting for transfers between devices: 1220 us -> 691 us
  blocking collectives: 0 us -> 110 us
  starting transfers between devices: 1.06 us -> 63.4 us
    all_gather x10 -> x0, waiting for transfers between devices: 689 us -> none  [settle(): lax.all_gather(solved.astype(jnp.bfloat16)[None], ('row', 'col'), axis=0,...]
    all_to_all x0 -> x7, waiting for transfers between devices: none -> 190 us  [settle(): pieces = jnp.concatenate(lax.all_to_all(sent, ('row', 'col'), 0, 0), axis=0)]
    all_to_all x0 -> x3, blocking collectives: none -> 110 us  [settle(): pieces = jnp.concatenate(lax.all_to_all(sent, ('row', 'col'), 0, 0), axis=0)]
    all_to_all x0 -> x7, starting transfers between devices: none -> 62.9 us  [settle(): pieces = jnp.concatenate(lax.all_to_all(sent, ('row', 'col'), 0, 0), axis=0)]
    unnamed x51 -> x43, local copies, waits for them, and re-layouts: 23.5 us -> 8.79 us
    reduce_scatter x5, waiting for transfers between devices: 162 us -> 149 us  [settle(): lax.psum_scatter(partial_value, 'col', scatter_dimension=2, tiled=True)]
    unnamed x26 -> x16, waiting for transfers between devices: 319 us -> 309 us
  transfers between devices with their start and end apart: 21 -> 18, of which waited for: 21 -> 18; matrix products, arithmetic and copies ran while one was open for 1% -> 2% of each run, Pallas kernels for 0% -> 0%
where the time goes in v1:
time: 970 us; the launch traced here: 967 us
  waiting for transfers between devices  691 us (71%)
  blocking collectives  110 us (11%)
  starting transfers between devices  63.4 us (7%)
  matrix products  40.3 us (4%)
  local copies, waits for them, and re-layouts  38 us (4%)
  between operations  14.9 us (2%)
    unnamed x16, waiting for transfers between devices  309 us
    all_to_all x7, waiting for transfers between devices, settle(): pieces = jnp.concatenate(lax.all_to_all(sent, ('row', 'col'), 0, 0), axis=0)  190 us
    reduce_scatter x5, waiting for transfers between devices, settle(): lax.psum_scatter(partial_value, 'col', scatter_dimension=2, tiled=True)  149 us
    all_to_all x3, blocking collectives, settle(): pieces = jnp.concatenate(lax.all_to_all(sent, ('row', 'col'), 0, 0), axis=0)  110 us
    all_to_all x7, starting transfers between devices, settle(): pieces = jnp.concatenate(lax.all_to_all(sent, ('row', 'col'), 0, 0), axis=0)  62.9 us
    psum x1, waiting for transfers between devices, shards(): coupling = lax.psum(coupling, 'leaf')  43.7 us
  transfers between devices with their start and end apart: 18, of which 18 were waited for; matrix products, arithmetic and copies ran while one was open for 2% of the time, Pallas kernels for 0%

profile of v1, /device:TPU:8, one launch (start us, length us, event | category | flops | bytes accessed | tf_op | source)
XLA Modules:
  0.0 967.4 jit_solution(13038042623170762899)
XLA Ops:
  7.2 1.2 copy-done
  9.5 1.7 bitcast_convert_fusion.9
  12.3 12.2 %all-to-all-start = ((bf16[64,1,1,256,32]{3,4,2,1,0:T(8,128)(2,1)}), bf16[64,1,1,256,32]{3,4,2,1,0:T(8,128)(2,1)}, u32[]{:S(2)}, u32[]{:S(2)}) async-start(bf16[64,1,1,256,32]{3,4,2,1,0:T(8,128)(2,1)} %stack.110), calls=%async_computation | async-start | bytes 2097152 | tf_op jit(solution)/shard_map/all_to_all | solution.py:22
  24.6 1.8 bitcast_multiply_fusion
  26.4 26.8 %all-to-all-done = bf16[64,1,1,256,32]{3,4,2,1,0:T(8,128)(2,1)} async-done(((bf16[64,1,1,256,32]{3,4,2,1,0:T(8,128)(2,1)}), bf16[64,1,1,256,32]{3,4,2,1,0:T(8,128)(2,1)}, u32[]{:S(2)}, u32[]{:S(2)}) %all-to-all-start) | async-done | bytes 1048608 | tf_op jit(solution)/shard_map/all_to_all | solution.py:22
  55.2 1.7 fusion.99
  56.9 1.6 copy.137
  58.5 1.3 dynamic-slice.1
  60.4 56.8 %all-reduce.14.cloned.1.call-done = f32[1,256,256]{1,0,2:T(1,128)} async-done(((f32[1,256,256]{1,0,2:T(1,128)}), f32[1,256,256]{1,0,2:T(1,128)}) %all-reduce.14.cloned.1.call-update) | async-done | bytes 262160
  118.0 1.7 bitcast_convert_fusion.8
  120.8 8.5 all-to-all-start.1
  130.1 27.9 %all-to-all-done.1 = bf16[64,1,1,256,32]{3,4,2,1,0:T(8,128)(2,1)} async-done(((bf16[64,1,1,256,32]{3,4,2,1,0:T(8,128)(2,1)}), bf16[64,1,1,256,32]{3,4,2,1,0:T(8,128)(2,1)}, u32[]{:S(2)}, u32[]{:S(2)}) %all-to-all-start.1) | async-done | bytes 1048608 | tf_op jit(solution)/shard_map/all_to_all | solution.py:22
  159.7 1.9 convolution_bitcast_fusion.8
  161.5 1.8 copy.89
  163.5 61.8 %all-reduce.16.cloned.1.call-done = f32[1,256,256]{1,0,2:T(1,128)} async-done(((f32[1,256,256]{1,0,2:T(1,128)}), f32[1,256,256]{1,0,2:T(1,128)}) %all-reduce.16.cloned.1.call-update) | async-done | bytes 262160
  226.0 1.7 bitcast_convert_fusion.7
  227.8 36.9 %all_to_all.50 = bf16[64,1,1,256,32]{3,4,2,1,0:T(8,128)(2,1)S(1)} all-to-all(bf16[64,1,1,256,32]{3,4,2,1,0:T(8,128)(2,1)S(1)} %stack.115), channel_id=1, replica_groups=mesh['leaf'=4,'row'=8,'col'=8] {'row','col'}, dimensions={0} | all-to-all | bytes 2097152 | tf_op jit(solution)/shard_map/all_to_all | solution.py:22
  265.5 1.9 convolution_bitcast_fusion.7
  267.4 1.8 copy.92
  269.3 61.8 %all-reduce.18.cloned.1.call-done = f32[1,256,256]{1,0,2:T(1,128)} async-done(((f32[1,256,256]{1,0,2:T(1,128)}), f32[1,256,256]{1,0,2:T(1,128)}) %all-reduce.18.cloned.1.call-update) | async-done | bytes 262160
  331.9 1.7 bitcast_convert_fusion.6
  334.7 8.5 all-to-all-start.3
  343.8 28.1 %all-to-all-done.3 = bf16[64,1,1,256,32]{3,4,2,1,0:T(8,128)(2,1)} async-done(((bf16[64,1,1,256,32]{3,4,2,1,0:T(8,128)(2,1)}), bf16[64,1,1,256,32]{3,4,2,1,0:T(8,128)(2,1)}, u32[]{:S(2)}, u32[]{:S(2)}) %all-to-all-start.3) | async-done | bytes 1048608 | tf_op jit(solution)/shard_map/all_to_all | solution.py:22
  373.5 2.5 convolution_bitcast_fusion
  376.2 43.7 %all-reduce.12.cloned.1.call-done = f32[2,1,256,256]{3,2,0,1:T(8,128)} async-done(((f32[2,1,256,256]{3,2,0,1:T(8,128)}), f32[2,1,256,256]{3,2,0,1:T(8,128)}) %all-reduce.12.cloned.1.call-update) | async-done | bytes 524304 | tf_op jit(solution)/shard_map/psum | solution.py:82
  421.7 1.1 constant_dynamic-slice_fusion.10
  422.9 66.2 %all-reduce.20.cloned.1.call-done = f32[1,256,256]{1,0,2:T(1,128)} async-done(((f32[1,256,256]{1,0,2:T(1,128)}), f32[1,256,256]{1,0,2:T(1,128)}) %all-reduce.20.cloned.1.call-update) | async-done | bytes 262160
  489.9 1.7 bitcast_convert_fusion.5
  492.7 8.5 all-to-all-start.4
  501.2 1.9 broadcast_multiply_fusion
  503.2 26.7 %all-to-all-done.4 = bf16[64,1,1,256,32]{3,4,2,1,0:T(8,128)(2,1)} async-done(((bf16[64,1,1,256,32]{3,4,2,1,0:T(8,128)(2,1)}), bf16[64,1,1,256,32]{3,4,2,1,0:T(8,128)(2,1)}, u32[]{:S(2)}, u32[]{:S(2)}) %all-to-all-start.4) | async-done | bytes 1048608 | tf_op jit(solution)/shard_map/all_to_all | solution.py:22
  529.9 1.3 fusion.1
  532.1 61.8 %all-reduce.22.cloned.1.call-done = f32[1,256,256]{1,0,2:T(1,128)} async-done(((f32[1,256,256]{1,0,2:T(1,128)}), f32[1,256,256]{1,0,2:T(1,128)}) %all-reduce.22.cloned.1.call-update) | async-done | bytes 262160
  594.7 1.9 bitcast_convert_fusion.4
  596.7 36.9 %all_to_all.51 = bf16[64,1,1,256,32]{3,4,2,1,0:T(8,128)(2,1)S(1)} all-to-all(bf16[64,1,1,256,32]{3,4,2,1,0:T(8,128)(2,1)S(1)} %stack.122), channel_id=1, replica_groups=mesh['leaf'=4,'row'=8,'col'=8] {'row','col'}, dimensions={0} | all-to-all | bytes 2097152 | tf_op jit(solution)/shard_map/all_to_all | solution.py:22
  633.6 1.8 convolution_bitcast_fusion.9
  635.5 29.9 %reduce-scatter.6.cloned.1.call-done = f32[1,256,32]{1,2,0:T(8,128)} async-done(((f32[1,256,256]{1,2,0:T(8,128)}), f32[1,256,32]{1,2,0:T(8,128)}) %reduce-scatter.6.cloned.1.call-update) | async-done | bytes 32784 | tf_op jit(solution)/shard_map/reduce_scatter | solution.py:17
  665.4 1.7 bitcast_convert_fusion.3
  667.1 1.1 stack.123
  668.2 8.4 all-to-all-start.6
  676.8 2.4 bitcast_multiply_fusion.3
  679.2 26.1 %all-to-all-done.6 = bf16[64,1,1,256,32]{3,4,2,1,0:T(8,128)(2,1)} async-done(((bf16[64,1,1,256,32]{3,4,2,1,0:T(8,128)(2,1)}), bf16[64,1,1,256,32]{3,4,2,1,0:T(8,128)(2,1)}, u32[]{:S(2)}, u32[]{:S(2)}) %all-to-all-start.6) | async-done | bytes 1048608 | tf_op jit(solution)/shard_map/all_to_all | solution.py:22
  706.3 1.9 convolution_bitcast_fusion.3
  708.3 29.9 %reduce-scatter.8.cloned.1.call-done = f32[1,256,32]{1,2,0:T(8,128)} async-done(((f32[1,256,256]{1,2,0:T(8,128)}), f32[1,256,32]{1,2,0:T(8,128)}) %reduce-scatter.8.cloned.1.call-update) | async-done | bytes 32784 | tf_op jit(solution)/shard_map/reduce_scatter | solution.py:17
  738.2 1.7 bitcast_convert_fusion.2
  739.9 1.1 stack.127
  741.1 8.5 all-to-all-start.7
  749.7 1.9 convolution_bitcast_fusion.4
  751.6 26.7 %all-to-all-done.7 = bf16[64,1,1,256,32]{3,4,2,1,0:T(8,128)(2,1)} async-done(((bf16[64,1,1,256,32]{3,4,2,1,0:T(8,128)(2,1)}), bf16[64,1,1,256,32]{3,4,2,1,0:T(8,128)(2,1)}, u32[]{:S(2)}, u32[]{:S(2)}) %all-to-all-start.7) | async-done | bytes 1048608 | tf_op jit(solution)/shard_map/all_to_all | solution.py:22
  779.2 1.9 fusion
  781.1 29.9 %reduce-scatter.10.cloned.1.call-done = f32[1,256,32]{1,2,0:T(8,128)} async-done(((f32[1,256,256]{1,2,0:T(8,128)}), f32[1,256,32]{1,2,0:T(8,128)}) %reduce-scatter.10.cloned.1.call-update) | async-done | bytes 32784 | tf_op jit(solution)/shard_map/reduce_scatter | solution.py:17
  811.0 1.7 bitcast_convert_fusion.1
  812.7 1.1 stack.128
  813.9 8.4 all-to-all-start.8
  823.0 27.9 %all-to-all-done.8 = bf16[64,1,1,256,32]{3,4,2,1,0:T(8,128)(2,1)} async-done(((bf16[64,1,1,256,32]{3,4,2,1,0:T(8,128)(2,1)}), bf16[64,1,1,256,32]{3,4,2,1,0:T(8,128)(2,1)}, u32[]{:S(2)}, u32[]{:S(2)}) %all-to-all-start.8) | async-done | bytes 1048608 | tf_op jit(solution)/shard_map/all_to_all | solution.py:22
  852.6 1.2 convolution_bitcast_fusion.2
  853.8 1.9 fusion.5
  855.8 29.9 %reduce-scatter.12.cloned.1.call-done = f32[1,256,32]{1,2,0:T(8,128)} async-done(((f32[1,256,256]{1,2,0:T(8,128)}), f32[1,256,32]{1,2,0:T(8,128)}) %reduce-scatter.12.cloned.1.call-update) | async-done | bytes 32784 | tf_op jit(solution)/shard_map/reduce_scatter | solution.py:17
  885.8 1.7 bitcast_convert_fusion
  887.6 36.7 %all_to_all.52 = bf16[64,1,1,256,32]{3,4,2,1,0:T(8,128)(2,1)S(1)} all-to-all(bf16[64,1,1,256,32]{3,4,2,1,0:T(8,128)(2,1)S(1)} %stack.132), channel_id=1, replica_groups=mesh['leaf'=4,'row'=8,'col'=8] {'row','col'}, dimensions={0} | all-to-all | bytes 2097152 | tf_op jit(solution)/shard_map/all_to_all | solution.py:22
  925.0 1.4 convolution_bitcast_fusion.1
  926.4 1.9 fusion.3
  929.0 29.3 %reduce-scatter.14.cloned.1.call-done = f32[1,256,32]{1,2,0:T(8,128)} async-done(((f32[1,256,256]{1,2,0:T(8,128)}), f32[1,256,32]{1,2,0:T(8,128)}) %reduce-scatter.14.cloned.1.call-update) | async-done | bytes 32784 | tf_op jit(solution)/shard_map/reduce_scatter | solution.py:17
  959.4 1.5 maximum_bitcast_fusion.11
  (103 shorter events, 27.6 us)
Async XLA Ops:
  7.2 1.2 copy-start
  8.4 16.1 %copy-start.10 = (s32[1,4,1,4,1]{3,4,2,1,0:T(1,128)S(1)}, s32[1,4,1,4,1]{3,4,2,1,0:T(1,128)}, u32[]{:S(2)}) copy-start(s32[1,4,1,4,1]{3,4,2,1,0:T(1,128)} %param.22) | copy-start | bytes 196
  8.6 16.0 %copy-start.1 = (f32[1,4,1,256,32]{4,3,2,1,0:T(8,128)}, f32[1,4,1,256,32]{4,3,2,1,0:T(8,128)S(1)}, u32[]{:S(2)}) copy-start(f32[1,4,1,256,32]{4,3,2,1,0:T(8,128)S(1)} %constant_dynamic-slice_fusion.11) | copy-start | bytes 393220
  12.3 40.9 %all-to-all-start = ((bf16[64,1,1,256,32]{3,4,2,1,0:T(8,128)(2,1)}), bf16[64,1,1,256,32]{3,4,2,1,0:T(8,128)(2,1)}, u32[]{:S(2)}, u32[]{:S(2)}) async-start(bf16[64,1,1,256,32]{3,4,2,1,0:T(8,128)(2,1)} %stack.110), calls=%async_computation | async-start | bytes 2097152 | tf_op jit(solution)/shard_map/all_to_all | solution.py:22
  24.5 92.7 %all-reduce.14.cloned.1.call-start = ((), (), s32[]{:S(2)}) async-start(), calls=%async_computation.21 | async-start | bytes 524288
  120.8 37.2 %all-to-all-start.1 = ((bf16[64,1,1,256,32]{3,4,2,1,0:T(8,128)(2,1)}), bf16[64,1,1,256,32]{3,4,2,1,0:T(8,128)(2,1)}, u32[]{:S(2)}, u32[]{:S(2)}) async-start(bf16[64,1,1,256,32]{3,4,2,1,0:T(8,128)(2,1)} %stack.112), calls=%async_computation.1 | async-start | bytes 2097152 | tf_op jit(solution)/shard_map/all_to_all | solution.py:22
  129.3 96.0 %all-reduce.16.cloned.1.call-start = ((), (), s32[]{:S(2)}) async-start(), calls=%async_computation.22 | async-start | bytes 524288
  163.4 167.8 %all-reduce.18.cloned.1.call-start = ((), (), s32[]{:S(2)}) async-start(), calls=%async_computation.23 | async-start | bytes 524288
  163.5 102.0 %copy-start.4 = (bf16[1,256,256]{2,1,0:T(8,128)(2,1)S(1)}, bf16[1,256,256]{2,1,0:T(8,128)(2,1)}, u32[]{:S(2)}) copy-start(bf16[1,256,256]{2,1,0:T(8,128)(2,1)} %copy.85) | copy-start | bytes 393220
  267.4 75.8 %copy-start.11 = (s32[1,2,1,4,1]{3,4,2,1,0:T(1,128)S(1)}, s32[1,2,1,4,1]{3,4,2,1,0:T(1,128)}, u32[]{:S(2)}) copy-start(s32[1,2,1,4,1]{3,4,2,1,0:T(1,128)} %param.23) | copy-start | bytes 100
  269.3 104.2 %copy-start.5 = (bf16[1,256,256]{2,1,0:T(8,128)(2,1)S(1)}, bf16[1,256,256]{2,1,0:T(8,128)(2,1)}, u32[]{:S(2)}) copy-start(bf16[1,256,256]{2,1,0:T(8,128)(2,1)} %copy.88) | copy-start | bytes 393220
  334.7 37.2 %all-to-all-start.3 = ((bf16[64,1,1,256,32]{3,4,2,1,0:T(8,128)(2,1)}), bf16[64,1,1,256,32]{3,4,2,1,0:T(8,128)(2,1)}, u32[]{:S(2)}, u32[]{:S(2)}) async-start(bf16[64,1,1,256,32]{3,4,2,1,0:T(8,128)(2,1)} %stack.118), calls=%async_computation.3 | async-start | bytes 2097152 | tf_op jit(solution)/shard_map/all_to_all | solution.py:22
  343.2 76.7 %all-reduce.12.cloned.1.call-start = ((), (), s32[]{:S(2)}) async-start(), calls=%async_computation.15 | async-start | bytes 1048576 | tf_op jit(solution)/shard_map/psum | solution.py:82
  376.1 113.0 %all-reduce.20.cloned.1.call-start = ((), (), s32[]{:S(2)}) async-start(), calls=%async_computation.24 | async-start | bytes 524288
  421.7 79.5 %copy-start.12 = (s32[2,1,2,1]{2,3,1,0:T(1,128)S(1)}, s32[2,1,2,1]{2,3,1,0:T(1,128)}, u32[]{:S(2)}) copy-start(s32[2,1,2,1]{2,3,1,0:T(1,128)} %param.25) | copy-start | bytes 52
  492.7 37.2 %all-to-all-start.4 = ((bf16[64,1,1,256,32]{3,4,2,1,0:T(8,128)(2,1)}), bf16[64,1,1,256,32]{3,4,2,1,0:T(8,128)(2,1)}, u32[]{:S(2)}, u32[]{:S(2)}) async-start(bf16[64,1,1,256,32]{3,4,2,1,0:T(8,128)(2,1)} %stack.121), calls=%async_computation.4 | async-start | bytes 2097152 | tf_op jit(solution)/shard_map/all_to_all | solution.py:22
  501.1 92.8 %all-reduce.22.cloned.1.call-start = ((), (), s32[]{:S(2)}) async-start(), calls=%async_computation.25 | async-start | bytes 524288
  532.0 133.4 %reduce-scatter.6.cloned.1.call-start = ((), (), s32[]{:S(2)}) async-start(), calls=%async_computation.16 | async-start | bytes 294912 | tf_op jit(solution)/shard_map/reduce_scatter | solution.py:17
  596.6 68.8 %copy-start.3 = (f32[32,256]{1,0:T(8,128)S(1)}, f32[32,256]{1,0:T(8,128)}, u32[]{:S(2)}) copy-start(f32[32,256]{1,0:T(8,128)} %get-tuple-element.28) | copy-start | bytes 98308
  633.6 43.1 %copy-start.13 = (s32[1,4,1,2,1]{1,4,3,2,0:T(1,128)S(1)}, s32[1,4,1,2,1]{1,4,3,2,0:T(1,128)}, u32[]{:S(2)}) copy-start(s32[1,4,1,2,1]{1,4,3,2,0:T(1,128)} %param.24) | copy-start | bytes 100
  668.2 37.1 %all-to-all-start.6 = ((bf16[64,1,1,256,32]{3,4,2,1,0:T(8,128)(2,1)}), bf16[64,1,1,256,32]{3,4,2,1,0:T(8,128)(2,1)}, u32[]{:S(2)}, u32[]{:S(2)}) async-start(bf16[64,1,1,256,32]{3,4,2,1,0:T(8,128)(2,1)} %stack.123), calls=%async_computation.7 | async-start | bytes 2097152 | tf_op jit(solution)/shard_map/all_to_all | solution.py:22
  676.6 61.6 %reduce-scatter.8.cloned.1.call-start = ((), (), s32[]{:S(2)}) async-start(), calls=%async_computation.17 | async-start | bytes 294912 | tf_op jit(solution)/shard_map/reduce_scatter | solution.py:17
  741.1 37.3 %all-to-all-start.7 = ((bf16[64,1,1,256,32]{3,4,2,1,0:T(8,128)(2,1)}), bf16[64,1,1,256,32]{3,4,2,1,0:T(8,128)(2,1)}, u32[]{:S(2)}, u32[]{:S(2)}) async-start(bf16[64,1,1,256,32]{3,4,2,1,0:T(8,128)(2,1)} %stack.127), calls=%async_computation.9 | async-start | bytes 2097152 | tf_op jit(solution)/shard_map/all_to_all | solution.py:22
  749.6 61.4 %reduce-scatter.10.cloned.1.call-start = ((), (), s32[]{:S(2)}) async-start(), calls=%async_computation.18 | async-start | bytes 294912 | tf_op jit(solution)/shard_map/reduce_scatter | solution.py:17
  813.9 37.1 %all-to-all-start.8 = ((bf16[64,1,1,256,32]{3,4,2,1,0:T(8,128)(2,1)}), bf16[64,1,1,256,32]{3,4,2,1,0:T(8,128)(2,1)}, u32[]{:S(2)}, u32[]{:S(2)}) async-start(bf16[64,1,1,256,32]{3,4,2,1,0:T(8,128)(2,1)} %stack.128), calls=%async_computation.11 | async-start | bytes 2097152 | tf_op jit(solution)/shard_map/all_to_all | solution.py:22
  822.2 63.5 %reduce-scatter.12.cloned.1.call-start = ((), (), s32[]{:S(2)}) async-start(), calls=%async_computation.19 | async-start | bytes 294912 | tf_op jit(solution)/shard_map/reduce_scatter | solution.py:17
  852.6 33.2 %copy-start.2 = (f32[32,256]{1,0:T(8,128)S(1)}, f32[32,256]{1,0:T(8,128)}, u32[]{:S(2)}) copy-start(f32[32,256]{1,0:T(8,128)} %get-tuple-element.22) | copy-start | bytes 98308
  855.8 102.5 %reduce-scatter.14.cloned.1.call-start = ((), (), s32[]{:S(2)}) async-start(), calls=%async_computation.20 | async-start | bytes 294912 | tf_op jit(solution)/shard_map/reduce_scatter | solution.py:17
  925.0 3.3 copy-start.7
  925.0 3.4 copy-start.8
  925.0 33.3 %copy-start.6 = (f32[32,256]{1,0:T(8,128)S(1)}, f32[32,256]{1,0:T(8,128)}, u32[]{:S(2)}) copy-start(f32[32,256]{1,0:T(8,128)} %get-tuple-element.20) | copy-start | bytes 98308
  925.0 34.4 %copy-start.9 = (f32[32,256]{1,0:T(8,128)S(1)}, f32[32,256]{1,0:T(8,128)}, u32[]{:S(2)}) copy-start(f32[32,256]{1,0:T(8,128)} %get-tuple-element.34) | copy-start | bytes 98308
Sparse Core Ops, SparseCore 0:
  55.3 61.8 all-reduce.13
  163.5 61.7 all-reduce.15
  269.4 61.7 all-reduce.17
  376.2 43.6 all-reduce.11
  422.1 66.9 all-reduce.19
  532.1 61.7 all-reduce.21
  635.6 29.7 reduce-scatter.5
  708.4 29.7 reduce-scatter.7
  781.3 29.6 reduce-scatter.9
  855.9 29.7 reduce-scatter.11
  928.5 29.7 reduce-scatter.13
